TPU v7x, 32 devices: a whole 2x2x4 slice. The times are simulated.
32 devices in a mesh: tm: 8 (over z, x), row: 4 (over y, core).
Axes of the slice: x: 2, y: 2, z: 4, core: 2. Of those that a mesh axis runs over, the one named last changes fastest.
Arguments:
- coupling: bfloat16 [8, 4096, 2048], P('tm', 'row'), as said below
- row_scale: float32 [8, 4096], P('tm', 'row'), may hold values from 0.1 to 10
- block_mask: int32 [8, 32, 16], P('tm', 'row'), may hold values 0 or 1
- link_map: int32 [8, 16], P('tm'), may hold values from 0 to 15, each once within a row
- tile_order: int32 [16], replicated, may hold values from 0 to 15, each once
- link_diag: float32 [8, 2048], P('tm'), may hold values from 0.1 to 1
Outputs:
- schur_rows: float32 [8, 2048, 2048], P('tm', 'row')
- chain_complement: float32 [8, 3, 128, 128], P('tm')
Inputs may be any that keep to these rules, and one draw needn't show every extreme that they name: `coupling`: entries lie within 6 / sqrt(4096) of zero. Each row of link_map lists every linking block once. tile_order lists every linking block once.
All inputs are finite; a program needn't handle non-finite values. No bound on the sum of `block_mask` on one device may be relied on, other than what follows from the above.
Results may differ from a plain program's by a relative error of at most 0.0011.
Values may be sent and summed in bfloat16 or wider, within the bound.
No kernel may reach another device: no remote copies, remote signals or barrier semaphores. Data moves between devices by JAX's collectives and lax.ppermute only.
A program may use at most 128 MiB of HBM per device.

v0:
```python
import jax
import jax.numpy as jnp
from jax import lax
from jax.sharding import PartitionSpec as P

L = 2048
BLK = 128
HIGHEST = lax.Precision.HIGHEST


def join_segments(earlier_seg, later_seg):
    top_one, cross_one, bottom_one, empty_one = earlier_seg
    top_two, cross_two, bottom_two, empty_two = later_seg
    both_empty = empty_one * empty_two
    middle = bottom_one + top_two
    middle = 0.5 * (middle + middle.T) + both_empty * jnp.eye(middle.shape[0], dtype=jnp.float32)
    factor = jnp.linalg.cholesky(middle)
    half_width = top_one.shape[0]
    solved = jax.scipy.linalg.cho_solve(
        (factor, True), jnp.concatenate([cross_one.T, cross_two], axis=1)
    )
    solve_one = solved[:, :half_width]
    solve_two = solved[:, half_width:]
    top_new = top_one - jnp.dot(cross_one, solve_one, precision=HIGHEST)
    cross_new = -jnp.dot(cross_one, solve_two, precision=HIGHEST)
    bottom_new = bottom_two - jnp.dot(cross_two.T, solve_two, precision=HIGHEST)
    first_empty = empty_one > 0.5
    second_empty = empty_two > 0.5
    top_out = jnp.where(first_empty, top_two, jnp.where(second_empty, top_one, top_new))
    cross_out = jnp.where(first_empty, cross_two, jnp.where(second_empty, cross_one, cross_new))
    bottom_out = jnp.where(first_empty, bottom_two, jnp.where(second_empty, bottom_one, bottom_new))
    return (top_out, cross_out, bottom_out, both_empty)


def contract_rows(left_cols, right_cols):
    return lax.dot_general(
        left_cols, right_cols, (((0,), (0,)), ((), ())), preferred_element_type=jnp.float32
    )


def local(coupling, row_scale, block_mask, link_map, tile_order, link_diag):
    local_slab = coupling[0]
    row_weights = row_scale[0]
    live_blocks = block_mask[0]
    block_map = link_map[0]
    diagonal = link_diag[0]
    slab_height = local_slab.shape[0]
    block_count = L // BLK
    owners = lax.axis_size("row")
    own_blocks = block_count // owners
    own_rows = own_blocks * BLK
    my_index = lax.axis_index("row")
    masked = (
        local_slab.reshape(slab_height // BLK, BLK, block_count, BLK)
        * live_blocks.astype(jnp.bfloat16)[:, None, :, None]
    ).reshape(slab_height, block_count, BLK)
    block_ids = jnp.arange(block_count, dtype=jnp.int32)
    source = jnp.sum(
        block_ids[None, :] * (block_map[None, :] == block_ids[:, None]).astype(jnp.int32), axis=1
    )
    global_cols = jnp.take(masked, source, axis=1).reshape(slab_height, L)
    my_blocks = lax.dynamic_slice_in_dim(tile_order, my_index * own_blocks, own_blocks)
    left_cols = jnp.take(masked, jnp.take(source, tile_order), axis=1).reshape(slab_height, L)
    scaled = (row_weights[:, None] * global_cols.astype(jnp.float32)).astype(jnp.bfloat16)
    owned = lax.psum_scatter(
        contract_rows(left_cols, scaled), "row", scatter_dimension=0, tiled=True
    )
    local_rows = jnp.arange(own_rows, dtype=jnp.int32)
    target = jnp.repeat(my_blocks, BLK) * BLK + local_rows % BLK
    column_ids = jnp.arange(L, dtype=jnp.int32)
    owned = owned + jnp.where(
        column_ids[None, :] == target[:, None], jnp.take(diagonal, target)[:, None], 0.0
    )

    def pick_rows(wanted):
        where_held = jnp.sum(block_ids * (tile_order == wanted).astype(jnp.int32))
        local_block = where_held - my_index * own_blocks
        is_held = (local_block >= 0) & (local_block < own_blocks)
        rows_here = lax.dynamic_slice_in_dim(
            owned, jnp.clip(local_block, 0, own_blocks - 1) * BLK, BLK
        )
        return jnp.where(is_held, rows_here, 0.0)

    first_rows = pick_rows(0)
    final_rows = pick_rows(block_count - 1)
    pieces = (first_rows[:, :BLK], first_rows[:, L - BLK :], final_rows[:, L - BLK :])
    summed = lax.psum((pieces[0], pieces[1], pieces[2]), "row")
    own_segment = (summed[0], summed[1], summed[2], jnp.zeros((), jnp.float32))
    stacked = jnp.stack(own_segment[:3])[None]
    every_segment = lax.all_gather(stacked, "tm", axis=0, tiled=True)
    segment_count = every_segment.shape[0]
    empty_flags = jnp.zeros((segment_count,), jnp.float32)
    prefixes = lax.associative_scan(
        jax.vmap(join_segments),
        (every_segment[:, 0], every_segment[:, 1], every_segment[:, 2], empty_flags),
    )
    position = lax.axis_index("tm")
    chain_out = jnp.stack(
        [lax.dynamic_index_in_dim(member, position, 0, False) for member in prefixes[:3]]
    )[None]
    return (owned[None], chain_out)


def solution(mesh):
    placed = (
        P("tm", "row", None),
        P("tm", "row"),
        P("tm", "row", None),
        P("tm", None),
        P(),
        P("tm", None),
    )
    return jax.shard_map(
        local,
        mesh=mesh,
        in_specs=placed,
        out_specs=(P("tm", "row", None), P("tm", None, None, None)),
        check_vma=False,
    )
```

profile of v0, /device:TPU:0, one launch (start us, length us, event | category | flops | bytes accessed | tf_op | source)
XLA Modules:
  0.0 581.4 jit_solution(10147022563122233437)
XLA Ops:
  7.2 6.4 %copy.204 = bf16[1,1024,2048]{1,2,0:T(8,128)(2,1)} copy(bf16[1,1024,2048]{2,1,0:T(8,128)(2,1)} %param.11) | data formatting | bytes 8388608 | tf_op args[0]
  13.6 6.4 %copy.206 = bf16[1024,16,128]{2,0,1:T(8,128)(2,1)} copy(bf16[1024,16,128]{0,2,1:T(8,128)(2,1)} %bitcast.199) | data formatting | bytes 8388608 | tf_op jit(solution)/shard_map/reshape;squeeze | solution.py:54
  21.7 5.8 %broadcast_multiply_fusion = bf16[1024,16,128]{2,0,1:T(8,128)(2,1)} fusion(bf16[1024,16,128]{2,0,1:T(8,128)(2,1)} %copy.206, bf16[1024,16]{0,1:T(8,128)(2,1)S(1)} %bitcast.215), kind=kLoop, calls=%fused_computation.8 | loop fusion | flops 2097152 | bytes 8421376 | tf_op jit(solution)/shard_map/mul | solution.py:54
  27.6 5.2 gather_fusion.2
  32.8 4.6 select_bitcast_fusion
  37.3 6.4 %copy.207 = bf16[1024,16,128]{0,2,1:T(8,128)(2,1)} copy(bf16[1024,16,128]{2,0,1:T(8,128)(2,1)} %select_bitcast_fusion) | data formatting | bytes 8388608 | tf_op jit(solution)/shard_map/jit(_take)/select_n | solution.py:63
  43.7 5.2 gather_fusion.3
  49.0 5.7 multiply_convert_fusion
  54.6 6.4 %copy.208 = bf16[1024,16,128]{0,2,1:T(8,128)(2,1)} copy(bf16[1024,16,128]{2,0,1:T(8,128)(2,1)} %multiply_convert_fusion) | data formatting | bytes 8388608 | tf_op jit(solution)/shard_map/convert_element_type | solution.py:64
  61.0 15.2 %fusion.103 = f32[2048,2048]{1,0:T(8,128)} fusion(bf16[1024,2048]{0,1:T(8,128)(2,1)} %bitcast.200, bf16[1024,2048]{0,1:T(8,128)(2,1)} %bitcast.201), kind=kOutput, calls=%fused_computation.217 | convolution fusion | flops 8589934592 | bytes 25165824 | tf_op jit(solution)/shard_map/dot_general | solution.py:36
  81.0 124.1 %reduce-scatter.2.cloned.1.call-done = f32[512,2048]{1,0:T(8,128)} async-done(((f32[2048,2048]{1,0:T(8,128)}), f32[512,2048]{1,0:T(8,128)}) %reduce-scatter.2.cloned.1.call-update) | async-done | bytes 4194320 | tf_op jit(solution)/shard_map/reduce_scatter | solution.py:65
  209.7 31.8 %all-reduce.21.cloned.1.call-done = (f32[1,128,128]{2,1,0:T(8,128)}, f32[1,128,128]{2,1,0:T(8,128)}, f32[1,128,128]{2,1,0:T(8,128)}) async-done(((f32[1,128,128]{2,1,0:T(8,128)}, f32[1,128,128]{2,1,0:T(8,128)}, f32[1,128,128]{2,1,0:T(8,128)}), (f32[1,128,128]{2,1,0:T(8,128)}, f32[1,128,128]{2,1,0:T(8,128)}, f32[1,128,128]{2,1,0:T(8,128)})) %all-reduce.21.cloned.1.call-update) | async-done | bytes 196624 | tf_op jit(solution)/shard_map/psum | solution.py:87
  243.1 4.8 fusion.113
  247.9 40.5 %all-gather.3.cloned.1.call-done = f32[24,128,128]{2,1,0:T(8,128)} async-done(((f32[3,128,128]{2,1,0:T(8,128)}), f32[24,128,128]{2,1,0:T(8,128)}) %all-gather.3.cloned.1.call-update) | async-done | bytes 1572880 | tf_op jit(solution)/shard_map/all_gather | solution.py:90
  291.0 46.9 %custom-call.41 = f32[4,128,128]{2,1,0:T(8,128)S(1)} custom-call(f32[4,128,128]{2,1,0:T(8,128)S(1)} %copy.216), custom_call_target="Cholesky" | custom-call | tf_op jit(solution)/shard_map/vmap(jit(cholesky))/cholesky | solution.py:17
  338.2 39.3 %custom-call.42 = f32[4,1,128,128]{2,3,1,0:T(8,128)S(1)} custom-call(f32[4,1,128,128]{3,2,1,0:T(8,128)S(1)} %select_bitcast_fusion.1), custom_call_target="InvertDiagBlocksLowerTriangular" | custom-call | tf_op jit(solution)/shard_map/vmap(jit(_cho_solve))/triangular_solve | solution.py:19
  381.7 23.5 %custom-call.43 = f32[2,128,128]{2,1,0:T(8,128)S(1)} custom-call(f32[2,128,128]{2,1,0:T(8,128)S(1)} %fusion.44), custom_call_target="Cholesky" | custom-call | tf_op jit(solution)/shard_map/vmap(jit(cholesky))/cholesky | solution.py:17
  405.4 28.4 %custom-call.44 = f32[2,1,128,128]{2,3,1,0:T(8,128)S(1)} custom-call(f32[2,1,128,128]{3,2,1,0:T(8,128)S(1)} %select_bitcast_fusion.3), custom_call_target="InvertDiagBlocksLowerTriangular" | custom-call | tf_op jit(solution)/shard_map/vmap(jit(_cho_solve))/triangular_solve | solution.py:19
  436.7 11.7 %custom-call.49 = f32[1,128,128]{2,1,0:T(8,128)S(1)} custom-call(f32[1,128,128]{2,1,0:T(8,128)S(1)} %fusion.66), custom_call_target="Cholesky" | custom-call | tf_op jit(solution)/shard_map/vmap(jit(cholesky))/cholesky | solution.py:17
  449.8 9.8 %custom-call.50 = f32[1,1,128,128]{2,3,1,0:T(8,128)S(1)} custom-call(f32[1,1,128,128]{3,2,1,0:T(8,128)S(1)} %fusion.48), custom_call_target="InvertDiagBlocksLowerTriangular" | custom-call | tf_op jit(solution)/shard_map/vmap(jit(_cho_solve))/triangular_solve | solution.py:19
  463.1 11.9 %custom-call.51 = f32[1,128,128]{2,1,0:T(8,128)S(1)} custom-call(f32[1,128,128]{2,1,0:T(8,128)S(1)} %fusion.59), custom_call_target="Cholesky" | custom-call | tf_op jit(solution)/shard_map/vmap(jit(cholesky))/cholesky | solution.py:17
  476.2 9.8 %custom-call.52 = f32[1,1,128,128]{2,3,1,0:T(8,128)S(1)} custom-call(f32[1,1,128,128]{3,2,1,0:T(8,128)S(1)} %fusion.49), custom_call_target="InvertDiagBlocksLowerTriangular" | custom-call | tf_op jit(solution)/shard_map/vmap(jit(_cho_solve))/triangular_solve | solution.py:19
  494.5 35.2 %custom-call.45 = f32[3,128,128]{2,1,0:T(8,128)S(1)} custom-call(f32[3,128,128]{2,1,0:T(8,128)S(1)} %fusion.30), custom_call_target="Cholesky" | custom-call | tf_op jit(solution)/shard_map/vmap(jit(cholesky))/cholesky | solution.py:17
  531.4 29.5 %custom-call.46 = f32[3,1,128,128]{2,3,1,0:T(8,128)S(1)} custom-call(f32[3,1,128,128]{3,2,1,0:T(8,128)S(1)} %select_bitcast_fusion.2), custom_call_target="InvertDiagBlocksLowerTriangular" | custom-call | tf_op jit(solution)/shard_map/vmap(jit(_cho_solve))/triangular_solve | solution.py:19
  (177 shorter events, 50.6 us)
Async XLA Ops:
  7.2 70.6 %copy-start = (f32[1,2048]{1,0:T(1,128)S(1)}, f32[1,2048]{1,0:T(1,128)}, u32[]{:S(2)}) copy-start(f32[1,2048]{1,0:T(1,128)} %param.16) | copy-start | bytes 24580
  7.2 198.0 %reduce-scatter.2.cloned.1.call-start = ((), (), s32[]{:S(2)}) async-start(), calls=%async_computation.1 | async-start | bytes 20971520 | tf_op jit(solution)/shard_map/reduce_scatter | solution.py:65
  13.6 6.4 %copy-start.7 = (s32[1,8,16]{2,1,0:T(8,128)S(1)}, s32[1,8,16]{2,1,0:T(8,128)}, u32[]{:S(2)}) copy-start(s32[1,8,16]{2,1,0:T(8,128)} %param.13) | copy-start | bytes 1540
  13.6 6.6 %copy-start.9 = (s32[1,16]{1,0:T(1,128)S(1)}, s32[1,16]{1,0:T(1,128)}, u32[]{:S(2)}) copy-start(s32[1,16]{1,0:T(1,128)} %param.14) | copy-start | bytes 196
  13.6 6.8 %copy-start.8 = (s32[16]{0:T(128)S(1)}, s32[16]{0:T(128)}, u32[]{:S(2)}) copy-start(s32[16]{0:T(128)} %param.15) | copy-start | bytes 196
  43.7 5.2 copy-start.6
  76.2 165.3 %all-reduce.21.cloned.1.call-start = ((), (), s32[]{:S(2)}) async-start(), calls=%async_computation.3 | async-start | bytes 393216 | tf_op jit(solution)/shard_map/psum | solution.py:87
  209.4 79.1 %all-gather.3.cloned.1.call-start = ((), (), s32[]{:S(2)}) async-start(), calls=%async_computation.2 | async-start | bytes 1769472 | tf_op jit(solution)/shard_map/all_gather | solution.py:90
  243.1 162.1 %copy-start.3 = (pred[128,128]{1,0:T(8,128)(4,1)}, pred[128,128]{1,0:T(8,128)(4,1)S(1)}, u32[]{:S(2)}) copy-start(pred[128,128]{1,0:T(8,128)(4,1)S(1)} %iota_compare_fusion.3) | copy-start | bytes 49156
  243.1 162.2 %copy-start.1 = (pred[128,128]{1,0:T(8,128)(4,1)}, pred[128,128]{1,0:T(8,128)(4,1)S(1)}, u32[]{:S(2)}) copy-start(pred[128,128]{1,0:T(8,128)(4,1)S(1)} %iota_compare_fusion.4) | copy-start | bytes 49156
  493.0 71.2 %copy-start.4 = (f32[1,128,128]{2,1,0:T(8,128)S(1)}, f32[1,128,128]{2,1,0:T(8,128)}, u32[]{:S(2)}) copy-start(f32[1,128,128]{2,1,0:T(8,128)} %get-tuple-element.42) | copy-start | bytes 196612
  494.1 70.6 %copy-start.2 = (f32[1,128,128]{1,2,0:T(8,128)S(1)}, f32[1,128,128]{1,2,0:T(8,128)}, u32[]{:S(2)}) copy-start(f32[1,128,128]{1,2,0:T(8,128)} %get-tuple-element.34) | copy-start | bytes 196612
  564.4 7.4 %copy-start.5 = (f32[1,1,128,128]{3,2,1,0:T(8,128)S(1)}, f32[1,1,128,128]{3,2,1,0:T(8,128)}, u32[]{:S(2)}) copy-start(f32[1,1,128,128]{3,2,1,0:T(8,128)} %get-tuple-element.22) | copy-start | bytes 196612
Sparse Core Ops, SparseCore 0:
  76.3 128.8 reduce-scatter.1
  209.5 31.9 all-reduce.20
  244.2 44.1 all-gather.2
where the time goes:
time: 590 us; the launch traced here: 581 us
  other arithmetic  284 us (48%)
  waiting for transfers between devices  197 us (33%)
  local copies, waits for them, and re-layouts  57.1 us (10%)
  matrix products  26.8 us (5%)
  between operations  16.4 us (3%)
    another operation x16, other arithmetic, join_segments(): factor = jnp.linalg.cholesky(middle)  132 us
    reduce_scatter x1, waiting for transfers between devices, local(): lax.psum_scatter(contract_rows(left_cols, scaled), 'row', scatter_dimensi...  124 us
    another operation x11, other arithmetic, join_segments(): jax.scipy.linalg.cho_solve((factor, True), jnp.concatenate([cross_one.T,...  119 us
    all_gather x1, waiting for transfers between devices, local(): every_segment = lax.all_gather(stacked, 'tm', axis=0, tiled=True)  40.5 us
    psum x1, waiting for transfers between devices, local(): summed = lax.psum((pieces[0], pieces[1], pieces[2]), 'row')  31.8 us
    dot_general x1, matrix products, contract_rows(): lax.dot_general(left_cols, right_cols, (((0,), (0,)), ((), ())), preferre...  15.2 us
  transfers between devices with their start and end apart: 3, of which 3 were waited for; matrix products, arithmetic and copies ran while one was open for 1% of the time, Pallas kernels for 0%

commit v1 on v0

--- a/solution.py
+++ b/solution.py
@@ -6,6 +6,25 @@
 L = 2048
 BLK = 128
 HIGHEST = lax.Precision.HIGHEST
+
+
+def ring_gather(value, axis, dim):
+    size, mine, span = (lax.axis_size(axis), lax.axis_index(axis), value.shape[dim])
+    ahead = [(i, (i + 1) % size) for i in range(size)]
+    behind = [(i, (i - 1) % size) for i in range(size)]
+    out = jnp.zeros((*value.shape[:dim], size * span, *value.shape[dim + 1 :]), value.dtype)
+    out = lax.dynamic_update_slice_in_dim(out, value, mine * span, axis=dim)
+    from_left = from_right = value
+    middle = size // 2
+    for step in range(1, middle + 1):
+        from_left = lax.ppermute(from_left, axis, ahead)
+        out = lax.dynamic_update_slice_in_dim(out, from_left, (mine - step) % size * span, axis=dim)
+        if step < size - middle:
+            from_right = lax.ppermute(from_right, axis, behind)
+            out = lax.dynamic_update_slice_in_dim(
+                out, from_right, (mine + step) % size * span, axis=dim
+            )
+    return out
 
 
 def join_segments(earlier_seg, later_seg):
@@ -87,7 +106,7 @@
     summed = lax.psum((pieces[0], pieces[1], pieces[2]), "row")
     own_segment = (summed[0], summed[1], summed[2], jnp.zeros((), jnp.float32))
     stacked = jnp.stack(own_segment[:3])[None]
-    every_segment = lax.all_gather(stacked, "tm", axis=0, tiled=True)
+    every_segment = ring_gather(stacked, "tm", 0)
     segment_count = every_segment.shape[0]
     empty_flags = jnp.zeros((segment_count,), jnp.float32)
     prefixes = lax.associative_scan(

time: 590 us -> 623 us (1.056)
  waiting for transfers between devices: 197 us -> 172 us
  starting transfers between devices: 0.38 us -> 18.9 us
  local copies, waits for them, and re-layouts: 57.1 us -> 73.7 us
  matrix products: 26.8 us -> 38.1 us
  other arithmetic: 284 us -> 292 us
    all_gather x1 -> x0, waiting for transfers between devices: 40.5 us -> none  [local(): every_segment = lax.all_gather(stacked, 'tm', axis=0, tiled=True)]
    ppermute x0 -> x7, starting transfers between devices: none -> 18.8 us  [the longest x3 9.63 us: ring_gather(): from_right = lax.ppermute(from_right, axis, behind)]
    ppermute x0 -> x7, waiting for transfers between devices: none -> 15.5 us  [the longest x4 14 us: ring_gather(): from_left = lax.ppermute(from_left, axis, ahead)]
    unnamed x40 -> x62, local copies, waits for them, and re-layouts: 10.7 us -> 17.2 us
    another operation x11, other arithmetic: 119 us -> 113 us  [join_segments(): jax.scipy.linalg.cho_solve((factor, True), jnp.concatenate([cross_one.T,...]
  transfers between devices with their start and end apart: 3 -> 9, of which waited for: 3 -> 7; matrix products, arithmetic and copies ran while one was open for 1% -> 1% of each run, Pallas kernels for 0% -> 0%
where the time goes in v1:
time: 623 us; the launch traced here: 611 us
  other arithmetic  292 us (47%)
  waiting for transfers between devices  172 us (28%)
  local copies, waits for them, and re-layouts  73.7 us (12%)
  matrix products  38.1 us (6%)
  starting transfers between devices  18.9 us (3%)
  between operations  16.9 us (3%)
    another operation x16, other arithmetic, join_segments(): factor = jnp.linalg.cholesky(middle)  135 us
    reduce_scatter x1, waiting for transfers between devices, local(): lax.psum_scatter(contract_rows(left_cols, scaled), 'row', scatter_dimensi...  124 us
    another operation x11, other arithmetic, join_segments(): jax.scipy.linalg.cho_solve((factor, True), jnp.concatenate([cross_one.T,...  113 us
    psum x1, waiting for transfers between devices, local(): summed = lax.psum((pieces[0], pieces[1], pieces[2]), 'row')  32.1 us
    unnamed x62, local copies, waits for them, and re-layouts  17.2 us
    dot_general x1, matrix products, contract_rows(): lax.dot_general(left_cols, right_cols, (((0,), (0,)), ((), ())), preferre...  15.3 us
    ppermute x4, waiting for transfers between devices, ring_gather(): from_left = lax.ppermute(from_left, axis, ahead)  14 us
  transfers between devices with their start and end apart: 9, of which 7 were waited for; matrix products, arithmetic and copies ran while one was open for 1% of the time, Pallas kernels for 0%

profile of v1, /device:TPU:0, one launch (start us, length us, event | category | flops | bytes accessed | tf_op | source)
XLA Modules:
  0.0 611.3 jit_solution(3872235796368012731)
XLA Ops:
  7.2 6.4 %copy.149 = bf16[1,1024,2048]{1,2,0:T(8,128)(2,1)} copy(bf16[1,1024,2048]{2,1,0:T(8,128)(2,1)} %param.11) | data formatting | bytes 8388608 | tf_op args[0]
  13.6 6.4 %copy.151 = bf16[1024,16,128]{2,0,1:T(8,128)(2,1)} copy(bf16[1024,16,128]{0,2,1:T(8,128)(2,1)} %bitcast.204) | data formatting | bytes 8388608 | tf_op jit(solution)/shard_map/reshape;squeeze | solution.py:73
  21.8 5.8 broadcast_multiply_fusion
  27.6 5.2 gather_fusion.2
  32.8 4.6 select_bitcast_fusion
  37.4 6.4 %copy.152 = bf16[1024,16,128]{0,2,1:T(8,128)(2,1)} copy(bf16[1024,16,128]{2,0,1:T(8,128)(2,1)} %select_bitcast_fusion) | data formatting | bytes 8388608 | tf_op jit(solution)/shard_map/jit(_take)/select_n | solution.py:82
  43.8 5.2 gather_fusion.3
  49.1 5.7 multiply_convert_fusion
  54.7 6.4 %copy.153 = bf16[1024,16,128]{0,2,1:T(8,128)(2,1)} copy(bf16[1024,16,128]{2,0,1:T(8,128)(2,1)} %multiply_convert_fusion) | data formatting | bytes 8388608 | tf_op jit(solution)/shard_map/convert_element_type | solution.py:83
  61.1 15.3 %fusion.113 = f32[2048,2048]{1,0:T(8,128)} fusion(bf16[1024,2048]{0,1:T(8,128)(2,1)} %bitcast.205, bf16[1024,2048]{0,1:T(8,128)(2,1)} %bitcast.206), kind=kOutput, calls=%fused_computation.231 | convolution fusion | flops 8589934592 | bytes 25165824 | tf_op jit(solution)/shard_map/dot_general | solution.py:55
  81.5 124.0 %reduce-scatter.2.cloned.1.call-done = f32[512,2048]{1,0:T(8,128)} async-done(((f32[2048,2048]{1,0:T(8,128)}), f32[512,2048]{1,0:T(8,128)}) %reduce-scatter.2.cloned.1.call-update) | async-done | bytes 4194320 | tf_op jit(solution)/shard_map/reduce_scatter | solution.py:84
  209.6 32.1 %all-reduce.21.cloned.1.call-done = (f32[1,128,128]{2,1,0:T(8,128)}, f32[1,128,128]{2,1,0:T(8,128)}, f32[1,128,128]{2,1,0:T(8,128)}) async-done(((f32[1,128,128]{2,1,0:T(8,128)}, f32[1,128,128]{2,1,0:T(8,128)}, f32[1,128,128]{2,1,0:T(8,128)}), (f32[1,128,128]{2,1,0:T(8,128)}, f32[1,128,128]{2,1,0:T(8,128)}, f32[1,128,128]{2,1,0:T(8,128)})) %all-reduce.21.cloned.1.call-update) | async-done | bytes 196624 | tf_op jit(solution)/shard_map/psum | solution.py:106
  247.4 4.8 fusion.123
  276.0 6.1 %collective-permute-done.6 = f32[1,3,128,128]{3,2,0,1:T(8,128)S(1)} collective-permute-done((f32[1,3,128,128]{3,2,0,1:T(8,128)S(1)}, f32[1,3,128,128]{3,2,0,1:T(8,128)S(1)}, u32[]{:S(2)}, u32[]{:S(2)}) %collective-permute-start.6) | collective-permute-done | bytes 196640 | tf_op jit(solution)/shard_map/ppermute | solution.py:20
  292.7 47.7 %custom-call.41 = f32[4,128,128]{2,1,0:T(8,128)S(1)} custom-call(f32[4,128,128]{2,1,0:T(8,128)} %copy.159), custom_call_target="Cholesky" | custom-call | tf_op jit(solution)/shard_map/vmap(jit(cholesky))/cholesky | solution.py:36
  340.7 39.3 %custom-call.42 = f32[4,1,128,128]{2,3,1,0:T(8,128)S(1)} custom-call(f32[4,1,128,128]{3,2,1,0:T(8,128)S(1)} %select_bitcast_fusion.1), custom_call_target="InvertDiagBlocksLowerTriangular" | custom-call | tf_op jit(solution)/shard_map/vmap(jit(_cho_solve))/triangular_solve | solution.py:38
  394.1 24.3 %custom-call.43 = f32[2,128,128]{2,1,0:T(8,128)S(1)} custom-call(f32[2,128,128]{2,1,0:T(8,128)} %fusion.51), custom_call_target="Cholesky" | custom-call | tf_op jit(solution)/shard_map/vmap(jit(cholesky))/cholesky | solution.py:36
  420.7 20.7 %custom-call.44 = f32[2,1,128,128]{2,3,1,0:T(8,128)S(1)} custom-call(f32[2,1,128,128]{3,2,1,0:T(8,128)} %select_bitcast_fusion.3), custom_call_target="InvertDiagBlocksLowerTriangular" | custom-call | tf_op jit(solution)/shard_map/vmap(jit(_cho_solve))/triangular_solve | solution.py:38
  452.0 11.7 %custom-call.49 = f32[1,128,128]{2,1,0:T(8,128)S(1)} custom-call(f32[1,128,128]{2,1,0:T(8,128)S(1)} %fusion.73), custom_call_target="Cholesky" | custom-call | tf_op jit(solution)/shard_map/vmap(jit(cholesky))/cholesky | solution.py:36
  465.0 9.8 %custom-call.50 = f32[1,1,128,128]{2,3,1,0:T(8,128)S(1)} custom-call(f32[1,1,128,128]{3,2,1,0:T(8,128)S(1)} %fusion.55), custom_call_target="InvertDiagBlocksLowerTriangular" | custom-call | tf_op jit(solution)/shard_map/vmap(jit(_cho_solve))/triangular_solve | solution.py:38
  488.7 12.7 %custom-call.51 = f32[1,128,128]{2,1,0:T(8,128)S(1)} custom-call(f32[1,128,128]{2,1,0:T(8,128)} %fusion.66), custom_call_target="Cholesky" | custom-call | tf_op jit(solution)/shard_map/vmap(jit(cholesky))/cholesky | solution.py:36
  502.8 9.8 %custom-call.52 = f32[1,1,128,128]{2,3,1,0:T(8,128)S(1)} custom-call(f32[1,1,128,128]{3,2,1,0:T(8,128)S(1)} %fusion.56), custom_call_target="InvertDiagBlocksLowerTriangular" | custom-call | tf_op jit(solution)/shard_map/vmap(jit(_cho_solve))/triangular_solve | solution.py:38
  523.6 35.2 %custom-call.45 = f32[3,128,128]{2,1,0:T(8,128)S(1)} custom-call(f32[3,128,128]{2,1,0:T(8,128)S(1)} %fusion.34), custom_call_target="Cholesky" | custom-call | tf_op jit(solution)/shard_map/vmap(jit(cholesky))/cholesky | solution.py:36
  560.4 29.5 %custom-call.46 = f32[3,1,128,128]{2,3,1,0:T(8,128)S(1)} custom-call(f32[3,1,128,128]{3,2,1,0:T(8,128)S(1)} %select_bitcast_fusion.2), custom_call_target="InvertDiagBlocksLowerTriangular" | custom-call | tf_op jit(solution)/shard_map/vmap(jit(_cho_solve))/triangular_solve | solution.py:38
  (224 shorter events, 119.4 us)
Async XLA Ops:
  7.2 70.9 %copy-start = (f32[1,2048]{1,0:T(1,128)S(1)}, f32[1,2048]{1,0:T(1,128)}, u32[]{:S(2)}) copy-start(f32[1,2048]{1,0:T(1,128)} %param.16) | copy-start | bytes 24580
  7.2 198.2 %reduce-scatter.2.cloned.1.call-start = ((), (), s32[]{:S(2)}) async-start(), calls=%async_computation.1 | async-start | bytes 20971520 | tf_op jit(solution)/shard_map/reduce_scatter | solution.py:84
  13.6 6.6 %copy-start.23 = (s32[1,16]{1,0:T(1,128)S(1)}, s32[1,16]{1,0:T(1,128)}, u32[]{:S(2)}) copy-start(s32[1,16]{1,0:T(1,128)} %param.14) | copy-start | bytes 196
  13.6 6.8 %copy-start.22 = (s32[16]{0:T(128)S(1)}, s32[16]{0:T(128)}, u32[]{:S(2)}) copy-start(s32[16]{0:T(128)} %param.15) | copy-start | bytes 196
  76.4 165.3 %all-reduce.21.cloned.1.call-start = ((), (), s32[]{:S(2)}) async-start(), calls=%async_computation.2 | async-start | bytes 393216 | tf_op jit(solution)/shard_map/psum | solution.py:106
  81.3 259.1 %copy-start.16 = (pred[128,128]{1,0:T(8,128)(4,1)}, pred[128,128]{1,0:T(8,128)(4,1)S(1)}, u32[]{:S(2)}) copy-start(pred[128,128]{1,0:T(8,128)(4,1)S(1)} %iota_compare_fusion.3) | copy-start | bytes 49156
  209.6 131.0 %copy-start.15 = (pred[128,128]{1,0:T(8,128)(4,1)}, pred[128,128]{1,0:T(8,128)(4,1)S(1)}, u32[]{:S(2)}) copy-start(pred[128,128]{1,0:T(8,128)(4,1)S(1)} %iota_compare_fusion.4) | copy-start | bytes 49156
  242.6 9.7 %copy-start.17 = (f32[1,128,128]{2,1,0:T(8,128)S(1)}, f32[1,128,128]{2,1,0:T(8,128)}, u32[]{:S(2)}) copy-start(f32[1,128,128]{2,1,0:T(8,128)} %get-tuple-element.15) | copy-start | bytes 196612
  242.6 9.7 %copy-start.18 = (f32[1,128,128]{2,1,0:T(8,128)S(1)}, f32[1,128,128]{2,1,0:T(8,128)}, u32[]{:S(2)}) copy-start(f32[1,128,128]{2,1,0:T(8,128)} %get-tuple-element.16) | copy-start | bytes 196612
  242.6 9.7 %copy-start.19 = (f32[1,128,128]{2,1,0:T(8,128)S(1)}, f32[1,128,128]{2,1,0:T(8,128)}, u32[]{:S(2)}) copy-start(f32[1,128,128]{2,1,0:T(8,128)} %get-tuple-element.17) | copy-start | bytes 196612
  242.6 9.8 %collective-permute-start = (f32[1,3,128,128]{3,2,0,1:T(8,128)S(1)}, f32[1,3,128,128]{3,2,0,1:T(8,128)S(1)}, u32[]{:S(2)}, u32[]{:S(2)}) collective-permute-start(f32[1,3,128,128]{3,2,0,1:T(8,128)S(1)} %maximum_bitcast_fusion), channel_id=1, source_target_pairs={{0,4},{4,8},{8,12},{12,16},{16,20},{20,24},{24,28},{28,0},{1,5},{5... | collective-permute-start | bytes 589832 | tf_op jit(solution)/shard_map/ppermute | solution.py:20
  244.2 10.3 %collective-permute-start.1 = (f32[1,3,128,128]{3,2,0,1:T(8,128)S(1)}, f32[1,3,128,128]{3,2,0,1:T(8,128)S(1)}, u32[]{:S(2)}, u32[]{:S(2)}) collective-permute-start(f32[1,3,128,128]{3,2,0,1:T(8,128)S(1)} %maximum_bitcast_fusion), channel_id=1, source_target_pairs={{0,28},{4,0},{8,4},{12,8},{16,12},{20,16},{24,20},{28,24},{1,29},{... | collective-permute-start | bytes 589832 | tf_op jit(solution)/shard_map/ppermute | solution.py:23
  252.4 10.1 %collective-permute-start.2 = (f32[1,3,128,128]{3,2,0,1:T(8,128)S(1)}, f32[1,3,128,128]{3,2,0,1:T(8,128)S(1)}, u32[]{:S(2)}, u32[]{:S(2)}) collective-permute-start(f32[1,3,128,128]{3,2,0,1:T(8,128)S(1)} %collective-permute-done), channel_id=1, source_target_pairs={{0,4},{4,8},{8,12},{12,16},{16,20},{20,24},{24,28},{28,0},{1,5},{5... | collective-permute-start | bytes 589832 | tf_op jit(solution)/shard_map/ppermute | solution.py:20
  254.5 11.0 %collective-permute-start.3 = (f32[1,3,128,128]{3,2,0,1:T(8,128)S(1)}, f32[1,3,128,128]{3,2,0,1:T(8,128)S(1)}, u32[]{:S(2)}, u32[]{:S(2)}) collective-permute-start(f32[1,3,128,128]{3,2,0,1:T(8,128)S(1)} %collective-permute-done.1), channel_id=1, source_target_pairs={{0,28},{4,0},{8,4},{12,8},{16,12},{20,16},{24,20},{28,24},{1,29},{... | collective-permute-start | bytes 589832 | tf_op jit(solution)/shard_map/ppermute | solution.py:23
  262.5 9.4 %collective-permute-start.4 = (f32[1,3,128,128]{3,2,0,1:T(8,128)S(1)}, f32[1,3,128,128]{3,2,0,1:T(8,128)S(1)}, u32[]{:S(2)}, u32[]{:S(2)}) collective-permute-start(f32[1,3,128,128]{3,2,0,1:T(8,128)S(1)} %collective-permute-done.2), channel_id=1, source_target_pairs={{0,4},{4,8},{8,12},{12,16},{16,20},{20,24},{24,28},{28,0},{1,5},{5... | collective-permute-start | bytes 589832 | tf_op jit(solution)/shard_map/ppermute | solution.py:20
  265.5 10.5 %collective-permute-start.5 = (f32[1,3,128,128]{3,2,0,1:T(8,128)S(1)}, f32[1,3,128,128]{3,2,0,1:T(8,128)S(1)}, u32[]{:S(2)}, u32[]{:S(2)}) collective-permute-start(f32[1,3,128,128]{3,2,0,1:T(8,128)S(1)} %collective-permute-done.3), channel_id=1, source_target_pairs={{0,28},{4,0},{8,4},{12,8},{16,12},{20,16},{24,20},{28,24},{1,29},{... | collective-permute-start | bytes 589832 | tf_op jit(solution)/shard_map/ppermute | solution.py:23
  271.9 10.3 %collective-permute-start.6 = (f32[1,3,128,128]{3,2,0,1:T(8,128)S(1)}, f32[1,3,128,128]{3,2,0,1:T(8,128)S(1)}, u32[]{:S(2)}, u32[]{:S(2)}) collective-permute-start(f32[1,3,128,128]{3,2,0,1:T(8,128)S(1)} %collective-permute-done.4), channel_id=1, source_target_pairs={{0,4},{4,8},{8,12},{12,16},{16,20},{20,24},{24,28},{28,0},{1,5},{5... | collective-permute-start | bytes 589832 | tf_op jit(solution)/shard_map/ppermute | solution.py:20
  287.2 92.8 %copy-start.5 = (f32[4,128,128]{1,2,0:T(8,128)S(1)}, f32[4,128,128]{1,2,0:T(8,128)}, u32[]{:S(2)}) copy-start(f32[4,128,128]{1,2,0:T(8,128)} %copy.220) | copy-start | bytes 786436
  384.6 56.8 %copy-start.1 = (f32[4,128,128]{1,2,0:T(8,128)}, f32[4,128,128]{1,2,0:T(8,128)S(1)}, u32[]{:S(2)}) copy-start(f32[4,128,128]{1,2,0:T(8,128)S(1)} %slice_subtract_fusion.1) | copy-start | bytes 786436
  477.7 39.9 %copy-start.8 = (f32[1,128,256]{2,1,0:T(8,128)}, f32[1,128,256]{2,1,0:T(8,128)S(1)}, u32[]{:S(2)}) copy-start(f32[1,128,256]{2,1,0:T(8,128)S(1)} %convolution_bitcast_fusion.1) | copy-start | bytes 393220
  522.0 71.9 %copy-start.3 = (f32[2,128,128]{2,1,0:T(8,128)S(1)}, f32[2,128,128]{2,1,0:T(8,128)}, u32[]{:S(2)}) copy-start(f32[2,128,128]{2,1,0:T(8,128)} %copy-done.2) | copy-start | bytes 393220
  522.0 71.9 %copy-start.7 = (f32[2,128,128]{2,1,0:T(8,128)S(1)}, f32[2,128,128]{2,1,0:T(8,128)}, u32[]{:S(2)}) copy-start(f32[2,128,128]{2,1,0:T(8,128)} %copy-done.6) | copy-start | bytes 393220
  522.0 71.9 %copy-start.9 = (f32[1,128,256]{2,1,0:T(8,128)S(1)}, f32[1,128,256]{2,1,0:T(8,128)}, u32[]{:S(2)}) copy-start(f32[1,128,256]{2,1,0:T(8,128)} %copy-done.8) | copy-start | bytes 393220
  522.0 73.1 %copy-start.11 = (f32[1,128,256]{2,1,0:T(8,128)S(1)}, f32[1,128,256]{2,1,0:T(8,128)}, u32[]{:S(2)}) copy-start(f32[1,128,256]{2,1,0:T(8,128)} %copy-done.10) | copy-start | bytes 393220
  (9 other events, 18.7 us)
Sparse Core Ops, SparseCore 0:
  76.6 128.8 reduce-scatter.1
  209.7 31.9 all-reduce.20
